TPU v7x, 128 devices: a whole 4x4x4 slice. The times are simulated.
128 devices in a mesh: rep: 4 (over x), fsdp: 2 (over core), tp: 16 (over z, y).
Axes of the slice: x: 4, y: 4, z: 4, core: 2. Of those that a mesh axis runs over, the one named last changes fastest.
Arguments:
- tokens: bfloat16 [8192, 2048], P(('rep', 'fsdp'), 'tp'), may hold values from -6 to 6
- cotangent: bfloat16 [8192, 2048], P(('rep', 'fsdp'), 'tp'), may hold values from -6 to 6
- frame_mask: int32 [8192], P(('rep', 'fsdp')), may hold values 0 or 1
- ln_gain: bfloat16 [2048], P('tp'), may hold values from 0.099609375 to 1.8984375
- ln_bias: bfloat16 [2048], P('tp'), may hold values from -3 to 3
- weight_in: bfloat16 [2048, 8192], P('fsdp', 'tp'), may hold values from -0.1875 to 0.1875
- weight_out: bfloat16 [8192, 2048], P('tp', 'fsdp'), may hold values from -0.09375 to 0.09375
- blocks_in: int32 [16, 64], P('fsdp', 'tp'), may hold values 0 or 1
- blocks_out: int32 [64, 16], P('tp', 'fsdp'), may hold values 0 or 1
Outputs:
- block_out: bfloat16 [8192, 2048], P(('rep', 'fsdp'), 'tp')
- input_grad: bfloat16 [8192, 2048], P(('rep', 'fsdp'), 'tp')
- grad_in: float32 [2048, 8192], P('fsdp', 'tp')
- grad_out: float32 [8192, 2048], P('tp', 'fsdp')
- grad_gain: float32 [2048], P('tp')
- grad_bias: float32 [2048], P('tp')
All inputs are finite; a program needn't handle non-finite values. No bound on the sum of `frame_mask` or of `blocks_in` or of `blocks_out` on one device may be relied on, other than what follows from the above.
Results may differ from a plain program's by a relative error of at most 0.019.
Values may be sent and summed in bfloat16 or wider, within the bound.
No kernel may reach another device: no remote copies, remote signals or barrier semaphores. Data moves between devices by JAX's collectives and lax.ppermute only.
A program may use at most 128 MiB of HBM per device.

v0:
```python
from functools import partial
import jax
import jax.numpy as jnp
from jax import lax
from jax.sharding import PartitionSpec as P

BLK = 128


def apply_blocks(weight, blocks, kind):
    row_blocks, col_blocks = blocks.shape
    shaped = weight.reshape(row_blocks, BLK, col_blocks, BLK)
    keeper = blocks.astype(kind)[:, None, :, None]
    return (shaped * keeper).reshape(weight.shape)


def contract_rows(left, right):
    return lax.dot_general(
        left, right, (((0,), (0,)), ((), ())), preferred_element_type=jnp.float32
    )


def contract_cols(left, right):
    return lax.dot_general(
        left, right, (((1,), (1,)), ((), ())), preferred_element_type=jnp.float32
    )


def on_device(
    tokens, cotangent, frame_mask, ln_gain, ln_bias, weight_in, weight_out, blocks_in, blocks_out
):
    whole_rows, whole_grad, gain_full, bias_full = (
        lax.all_gather(tokens, "tp", axis=1, tiled=True),
        lax.all_gather(cotangent, "tp", axis=1, tiled=True),
        lax.all_gather(ln_gain, "tp", axis=0, tiled=True),
        lax.all_gather(ln_bias, "tp", axis=0, tiled=True),
    )
    masked_in = apply_blocks(weight_in, blocks_in, jnp.bfloat16)
    masked_out = apply_blocks(weight_out, blocks_out, jnp.bfloat16)
    full_in, full_out = (
        lax.all_gather(masked_in, "fsdp", axis=0, tiled=True),
        lax.all_gather(masked_out, "fsdp", axis=1, tiled=True),
    )
    width = whole_rows.shape[1]
    own_width = tokens.shape[1]
    col_start = lax.axis_index("tp") * own_width
    gelu_exact = partial(jax.nn.gelu, approximate=False)
    values = whole_rows.astype(jnp.float32)
    centre = jnp.mean(values, axis=1, keepdims=True)
    centred = values - centre
    inv_std = lax.rsqrt(jnp.mean(centred * centred, axis=1, keepdims=True) + 1e-05)
    normed = centred * inv_std
    scaled = (normed * gain_full.astype(jnp.float32) + bias_full.astype(jnp.float32)).astype(
        jnp.bfloat16
    )
    hidden = jnp.dot(scaled, full_in, preferred_element_type=jnp.float32)
    active = gelu_exact(hidden).astype(jnp.bfloat16)
    partial_out = jnp.dot(active, full_out, preferred_element_type=jnp.float32)
    branch = lax.psum_scatter(
        partial_out.astype(jnp.bfloat16), "tp", scatter_dimension=1, tiled=True
    ).astype(jnp.float32)
    block_out = (tokens.astype(jnp.float32) + branch).astype(jnp.bfloat16)
    flags = frame_mask[:, None].astype(jnp.bfloat16)
    chosen = whole_grad * flags
    chosen_own = cotangent * flags
    back_active = contract_cols(chosen, full_out)
    unused, gelu_back = jax.vjp(gelu_exact, hidden)
    back_hidden = gelu_back(back_active)[0].astype(jnp.bfloat16)
    partial_normed = contract_cols(back_hidden, full_in)
    normed_own = lax.dynamic_slice_in_dim(normed, col_start, own_width, 1)
    gain_own = ln_gain.astype(jnp.float32)
    back_normed = lax.psum_scatter(
        partial_normed.astype(jnp.bfloat16), "tp", scatter_dimension=1, tiled=True
    ).astype(jnp.float32)
    back_scaled = back_normed * gain_own
    sum_plain = jnp.sum(back_scaled, axis=1)
    sum_cross = jnp.sum(back_scaled * normed_own, axis=1)
    sum_plain, sum_cross = lax.psum((sum_plain, sum_cross), "tp")
    mean_plain = (sum_plain / width)[:, None]
    mean_cross = (sum_cross / width)[:, None]
    back_rows = inv_std * (back_scaled - mean_plain - normed_own * mean_cross)
    input_grad = (chosen_own.astype(jnp.float32) + back_rows).astype(jnp.bfloat16)
    local_gain = jnp.sum(back_normed * normed_own, axis=0)
    local_bias = jnp.sum(back_normed, axis=0)
    grad_gain, grad_bias = lax.psum((local_gain, local_bias), ("rep", "fsdp"))
    term_in = contract_rows(scaled, back_hidden)
    term_out = contract_rows(active, chosen)
    shard_in, shard_out = (
        lax.psum_scatter(
            term_in.astype(jnp.bfloat16), "fsdp", scatter_dimension=0, tiled=True
        ).astype(jnp.float32),
        lax.psum_scatter(
            term_out.astype(jnp.bfloat16), "fsdp", scatter_dimension=1, tiled=True
        ).astype(jnp.float32),
    )
    shard_in, shard_out = (
        lax.psum(shard_in.astype(jnp.bfloat16), "rep").astype(jnp.float32),
        lax.psum(shard_out.astype(jnp.bfloat16), "rep").astype(jnp.float32),
    )
    grad_in = apply_blocks(shard_in, blocks_in, jnp.float32)
    grad_out = apply_blocks(shard_out, blocks_out, jnp.float32)
    return (block_out, input_grad, grad_in, grad_out, grad_gain, grad_bias)


def solution(mesh):
    placed = (
        P(("rep", "fsdp"), "tp"),
        P(("rep", "fsdp"), "tp"),
        P(("rep", "fsdp")),
        P("tp"),
        P("tp"),
        P("fsdp", "tp"),
        P("tp", "fsdp"),
        P("fsdp", "tp"),
        P("tp", "fsdp"),
    )
    return jax.shard_map(
        on_device,
        mesh=mesh,
        in_specs=placed,
        out_specs=(
            P(("rep", "fsdp"), "tp"),
            P(("rep", "fsdp"), "tp"),
            P("fsdp", "tp"),
            P("tp", "fsdp"),
            P("tp"),
            P("tp"),
        ),
        check_vma=False,
    )
```

profile of v0, /device:TPU:0, one launch (start us, length us, event | category | flops | bytes accessed | tf_op | source)
XLA Modules:
  0.0 492.1 jit_solution(3719068611543885792)
XLA Ops:
  7.2 0.0 all-gather.7.cloned.1.call-start
  7.2 0.7 all-gather.7.cloned.1.call-update
  7.9 0.0 all-gather.9.cloned.1.call-start
  7.9 0.8 fusion.34
  8.7 0.1 copy.17
  8.8 0.3 mul.149
  9.2 0.0 copy-start.2
  9.2 2.4 bitcast_multiply_fusion.3
  11.6 0.0 all-gather.9.cloned.1.call-update
  11.6 0.0 all-gather.11.cloned.1.call-start
  11.7 0.2 mul.155
  12.0 1.2 bitcast_multiply_fusion.2
  13.2 0.0 all-gather.11.cloned.1.call-update
  13.2 0.0 all-gather.13.cloned.1.call-start
  13.2 0.5 all-gather.13.cloned.1.call-update
  13.8 0.0 reduce-scatter.9.cloned.1.call-start
  13.8 22.1 %all-gather = bf16[16,1,128]{2,1,0:T(2,128)(2,1)S(1)} all-gather(bf16[1,1,128]{2,1,0:T(2,128)(2,1)S(1)} %bitcast.45), channel_id=1, replica_groups=mesh['rep'=4,'fsdp'=2,'tp'=16] {'tp'}, dimensions={0}, use_global_device_ids=true | all-gather | bytes 4352 | tf_op jit(solution)/shard_map/all_gather | solution.py:35
  36.0 19.5 %all-gather.1 = bf16[16,1,128]{2,1,0:T(2,128)(2,1)S(1)} all-gather(bf16[1,1,128]{2,1,0:T(2,128)(2,1)S(1)} %bitcast.44), channel_id=1, replica_groups=mesh['rep'=4,'fsdp'=2,'tp'=16] {'tp'}, dimensions={0}, use_global_device_ids=true | all-gather | bytes 4352 | tf_op jit(solution)/shard_map/all_gather | solution.py:36
  55.5 14.8 %all-gather.7.cloned.1.call-done = bf16[1024,2048]{1,0:T(8,128)(2,1)} async-done(((bf16[1024,128]{1,0:T(8,128)(2,1)}), bf16[1024,2048]{1,0:T(8,128)(2,1)}) %all-gather.7.cloned.1.call-update) | async-done | bytes 4194320 | tf_op jit(solution)/shard_map/all_gather | solution.py:33
  70.4 3.0 convert_reduce_fusion
  73.4 0.5 copy-done
  73.8 1.2 fusion.2
  75.1 10.1 %all-gather.9.cloned.1.call-done = bf16[2048,512]{1,0:T(8,128)(2,1)} async-done(((bf16[1024,512]{1,0:T(8,128)(2,1)}), bf16[2048,512]{1,0:T(8,128)(2,1)}) %all-gather.9.cloned.1.call-update) | async-done | bytes 2097168 | tf_op jit(solution)/shard_map/all_gather | solution.py:41
  85.1 10.5 %multiply_convert_fusion = (bf16[1024,512]{1,0:T(8,128)(2,1)S(1)}, f32[1024,512]{1,0:T(8,128)}, f32[1024,512]{1,0:T(8,128)}) fusion(bf16[2048,512]{1,0:T(8,128)(2,1)} %all-gather.9.cloned.1.call-done, f32[2048]{0:T(1024)S(1)} %bitcast.42, f32[2048]{0:T(1024)S(1)} %bitcast.40, f32[1024]{0:T(1024)S(1)} %add_rsqrt_fusion, ...), kind=kOutput, calls=%fused_computation.21 | convolution fusion | flops 2194145280 | bytes 11558912 | tf_op jit(solution)/shard_map/dot_general | solution.py:56
  95.6 5.8 %all-gather.11.cloned.1.call-done = bf16[512,2048]{1,0:T(8,128)(2,1)} async-done(((bf16[512,1024]{1,0:T(8,128)(2,1)}), bf16[512,2048]{1,0:T(8,128)(2,1)}) %all-gather.11.cloned.1.call-update) | async-done | bytes 2097168 | tf_op jit(solution)/shard_map/all_gather | solution.py:42
  101.4 61.1 %all-gather.13.cloned.1.call-done = bf16[1024,2048]{1,0:T(8,128)(2,1)} async-done(((bf16[1024,128]{1,0:T(8,128)(2,1)}), bf16[1024,2048]{1,0:T(8,128)(2,1)}) %all-gather.13.cloned.1.call-update) | async-done | bytes 4194320 | tf_op jit(solution)/shard_map/all_gather | solution.py:34
  162.5 7.1 %add_convert_fusion.1 = bf16[1024,512]{1,0:T(8,128)(2,1)S(1)} fusion(f32[1024,512]{1,0:T(8,128)} %get-tuple-element.17, f32[1024,512]{1,0:T(8,128)} %get-tuple-element.22, bf16[512,2048]{1,0:T(8,128)(2,1)} %all-gather.11.cloned.1.call-done, bf16[1024,2048]{1,0:T(8,128)(2,1)} %all-gather.13.cloned.1.call-done, bf16[1024]{0:T(1024)(128)(2,1)S(1)} %convert_element_type.88), kind=kOutput, calls=%fused_computation.18 | convolution fusion | flops 2156920832 | bytes 11536384 | tf_op jit(solution)/shard_map/dot_general | solution.py:24
  169.7 1.0 copy-done.14
  170.7 4.4 convolution_convert_fusion.2
  175.1 0.0 reduce-scatter.9.cloned.1.call-update
  175.1 0.2 reduce-scatter.11.cloned.1.call-start
  175.4 6.0 %fusion.7 = bf16[512,2048]{1,0:T(8,128)(2,1)} fusion(bf16[1024,512]{1,0:T(8,128)(2,1)S(1)} %get-tuple-element.16, bf16[1024,2048]{1,0:T(8,128)(2,1)} %all-gather.13.cloned.1.call-done, bf16[1024]{0:T(1024)(128)(2,1)S(1)} %convert_element_type.88), kind=kOutput, calls=%fused_computation.14 | convolution fusion | flops 2150629376 | bytes 7342080 | tf_op jit(solution)/shard_map/dot_general | solution.py:18
  181.3 0.0 reduce-scatter.11.cloned.1.call-update
  181.4 0.0 all-reduce.5.cloned.1.call-start
  181.4 5.3 %reduce-scatter.9.cloned.1.call-done = bf16[1024,512]{1,0:T(8,128)(2,1)} async-done(((bf16[2048,512]{1,0:T(8,128)(2,1)}), bf16[1024,512]{1,0:T(8,128)(2,1)}) %reduce-scatter.9.cloned.1.call-update) | async-done | bytes 1048592 | tf_op jit(solution)/shard_map/reduce_scatter | solution.py:89
  186.7 16.6 %reduce-scatter.11.cloned.1.call-done = bf16[512,1024]{1,0:T(8,128)(2,1)} async-done(((bf16[512,2048]{1,0:T(8,128)(2,1)}), bf16[512,1024]{1,0:T(8,128)(2,1)}) %reduce-scatter.11.cloned.1.call-update) | async-done | bytes 1048592 | tf_op jit(solution)/shard_map/reduce_scatter | solution.py:92
  203.3 0.0 all-reduce.5.cloned.1.call-update
  203.3 0.0 reduce-scatter.15.cloned.1.call-start
  203.4 5.5 %convolution_convert_fusion = bf16[1024,2048]{1,0:T(8,128)(2,1)} fusion(bf16[1024,512]{1,0:T(8,128)(2,1)} %copy-done.14, bf16[2048,512]{1,0:T(8,128)(2,1)S(1)} %copy-done.11), kind=kOutput, calls=%fused_computation.6 | convolution fusion | flops 2149580800 | bytes 7340032 | tf_op jit(solution)/shard_map/dot_general | solution.py:24
  208.9 6.4 %copy.21 = bf16[1024,2048]{0,1:T(8,128)(2,1)} copy(bf16[1024,2048]{1,0:T(8,128)(2,1)} %convolution_convert_fusion) | data formatting | bytes 8388608
  215.3 0.0 reduce-scatter.15.cloned.1.call-update
  215.3 0.0 reduce-scatter.13.cloned.1.call-start
  215.4 1.6 copy-done.12
  217.0 5.5 %convolution_convert_fusion.1 = bf16[1024,2048]{1,0:T(8,128)(2,1)} fusion(bf16[1024,512]{1,0:T(8,128)(2,1)} %copy-done.13, bf16[512,2048]{1,0:T(8,128)(2,1)S(1)} %copy-done.12), kind=kOutput, calls=%fused_computation.7 | convolution fusion | flops 2149580800 | bytes 7340032 | tf_op jit(solution)/shard_map/dot_general | solution.py:58
  222.5 6.4 %copy.19 = bf16[1024,2048]{0,1:T(8,128)(2,1)} copy(bf16[1024,2048]{1,0:T(8,128)(2,1)} %convolution_convert_fusion.1) | data formatting | bytes 8388608
  228.9 0.0 reduce-scatter.13.cloned.1.call-update
  228.9 0.1 copy.18
  229.0 6.4 %fusion = f32[1024,2048]{1,0:T(8,128)} fusion(bf16[1024,2048]{1,0:T(8,128)(2,1)} %all-gather.7.cloned.1.call-done, f32[1024]{0:T(1024)S(1)} %add_rsqrt_fusion, f32[1024]{0:T(1024)S(1)} %broadcast_multiply_fusion.2), kind=kLoop, calls=%fused_computation.2 | loop fusion | flops 6291456 | bytes 12591104 | tf_op jit(solution)/shard_map/mul | solution.py:52
  235.4 30.6 %all-reduce.5.cloned.1.call-done = (bf16[1024,512]{1,0:T(8,128)(2,1)}, bf16[512,1024]{1,0:T(8,128)(2,1)}) async-done(((bf16[1024,512]{1,0:T(8,128)(2,1)}, bf16[512,1024]{1,0:T(8,128)(2,1)}), (bf16[1024,512]{1,0:T(8,128)(2,1)}, bf16[512,1024]{1,0:T(8,128)(2,1)})) %all-reduce.5.cloned.1.call-update) | async-done | bytes 2097168 | tf_op jit(solution)/shard_map/psum | solution.py:97
  266.0 0.3 mul.177
  266.4 0.9 copy-done.4
  267.3 1.7 bitcast_multiply_fusion.1
  268.9 0.2 mul.180
  269.1 1.0 copy-done.3
  270.2 2.0 bitcast_multiply_fusion
  272.2 75.3 %reduce-scatter.15.cloned.1.call-done = bf16[128,1024]{1,0:T(8,128)(2,1)} async-done(((bf16[2048,1024]{1,0:T(8,128)(2,1)}), bf16[128,1024]{1,0:T(8,128)(2,1)}) %reduce-scatter.15.cloned.1.call-update) | async-done | bytes 262160
  347.4 1.1 copy.22
  348.5 79.2 %reduce-scatter.13.cloned.1.call-done = bf16[128,1024]{1,0:T(8,128)(2,1)} async-done(((bf16[2048,1024]{1,0:T(8,128)(2,1)}), bf16[128,1024]{1,0:T(8,128)(2,1)}) %reduce-scatter.13.cloned.1.call-update) | async-done | bytes 262160
  427.7 1.1 copy.20
  428.8 0.8 add_convert_fusion.4
  429.6 1.4 fusion.29
  431.0 13.5 %all-reduce.1 = (f32[128]{0:T(128)}, f32[128]{0:T(128)}) all-reduce(f32[128]{0:T(128)S(1)} %get-tuple-element.6, f32[128]{0:T(128)S(1)} %get-tuple-element.9), channel_id=1, replica_groups=mesh['rep'=4,'fsdp'=2,'tp'=16] {'rep','fsdp'}, use_global_device_ids=true, to_apply=%region_13.0 | all-reduce | flops 256 | bytes 2048 | tf_op jit(solution)/shard_map/psum | solution.py:85
  444.5 38.7 %all-reduce = (f32[1024]{0:T(1024)S(1)}, f32[1024]{0:T(1024)S(1)}) all-reduce(f32[1024]{0:T(1024)S(1)} %get-tuple-element.7, f32[1024]{0:T(1024)S(1)} %get-tuple-element.8), channel_id=1, replica_groups=mesh['rep'=4,'fsdp'=2,'tp'=16] {'tp'}, use_global_device_ids=true, to_apply=%region_7.0 | all-reduce | flops 2048 | bytes 16384 | tf_op jit(solution)/shard_map/psum | solution.py:78
  483.2 2.4 fusion.27
  (32 shorter events, 0.1 us)
Async XLA Ops:
  7.2 63.2 %all-gather.7.cloned.1.call-start = ((), (), s32[]{:S(2)}) async-start(), calls=%async_computation.4 | async-start | bytes 4456448 | tf_op jit(solution)/shard_map/all_gather | solution.py:33
  7.9 77.2 %all-gather.9.cloned.1.call-start = ((), (), s32[]{:S(2)}) async-start(), calls=%async_computation.5 | async-start | bytes 3145728 | tf_op jit(solution)/shard_map/all_gather | solution.py:41
  9.2 2.5 copy-start.8
  9.2 2.7 copy-start.2
  11.6 89.8 %all-gather.11.cloned.1.call-start = ((), (), s32[]{:S(2)}) async-start(), calls=%async_computation.6 | async-start | bytes 3145728 | tf_op jit(solution)/shard_map/all_gather | solution.py:42
  11.9 1.9 copy-start.10
  11.9 24.1 %copy-start.9 = (bf16[128]{0:T(256)(128)(2,1)S(1)}, bf16[128]{0:T(256)(128)(2,1)}, u32[]{:S(2)}) copy-start(bf16[128]{0:T(256)(128)(2,1)} %param.13) | copy-start | bytes 772
  11.9 43.6 %copy-start.7 = (s32[1024]{0:T(1024)S(1)}, s32[1024]{0:T(1024)}, u32[]{:S(2)}) copy-start(s32[1024]{0:T(1024)} %param.11) | copy-start | bytes 12292
  13.2 149.3 %all-gather.13.cloned.1.call-start = ((), (), s32[]{:S(2)}) async-start(), calls=%async_computation.7 | async-start | bytes 4456448 | tf_op jit(solution)/shard_map/all_gather | solution.py:34
  13.8 173.0 %reduce-scatter.9.cloned.1.call-start = ((), (), s32[]{:S(2)}) async-start(), calls=%async_computation.8 | async-start | bytes 3145728 | tf_op jit(solution)/shard_map/reduce_scatter | solution.py:89
  70.4 3.4 copy-start
  95.6 79.8 %copy-start.13 = (bf16[1024,512]{1,0:T(8,128)(2,1)}, bf16[1024,512]{1,0:T(8,128)(2,1)S(1)}, u32[]{:S(2)}) copy-start(bf16[1024,512]{1,0:T(8,128)(2,1)S(1)} %get-tuple-element.16) | copy-start | bytes 3145732
  162.5 8.1 %copy-start.1 = (bf16[1024,2048]{1,0:T(8,128)(2,1)S(1)}, bf16[1024,2048]{1,0:T(8,128)(2,1)}, u32[]{:S(2)}) copy-start(bf16[1024,2048]{1,0:T(8,128)(2,1)} %all-gather.7.cloned.1.call-done) | copy-start | bytes 12582916
  169.6 1.0 copy-start.14
  175.1 28.2 %reduce-scatter.11.cloned.1.call-start = ((), (), s32[]{:S(2)}) async-start(), calls=%async_computation.9 | async-start | bytes 3145728 | tf_op jit(solution)/shard_map/reduce_scatter | solution.py:92
  181.3 22.1 %copy-start.11 = (bf16[2048,512]{1,0:T(8,128)(2,1)S(1)}, bf16[2048,512]{1,0:T(8,128)(2,1)}, u32[]{:S(2)}) copy-start(bf16[2048,512]{1,0:T(8,128)(2,1)} %all-gather.9.cloned.1.call-done) | copy-start | bytes 6291460
  181.4 84.7 %all-reduce.5.cloned.1.call-start = ((), (), s32[]{:S(2)}) async-start(), calls=%async_computation.12 | async-start | bytes 4194304 | tf_op jit(solution)/shard_map/psum | solution.py:97
  203.3 144.1 %reduce-scatter.15.cloned.1.call-start = ((), (), s32[]{:S(2)}) async-start(), calls=%async_computation.11 | async-start | bytes 4456448
  215.3 1.6 copy-start.12
  215.3 212.4 %reduce-scatter.13.cloned.1.call-start = ((), (), s32[]{:S(2)}) async-start(), calls=%async_computation.10 | async-start | bytes 4456448
  266.0 1.2 copy-start.4
  268.9 1.2 copy-start.3
  270.2 158.7 %copy-start.5 = (bf16[1024,128]{1,0:T(8,128)(2,1)S(1)}, bf16[1024,128]{1,0:T(8,128)(2,1)}, u32[]{:S(2)}) copy-start(bf16[1024,128]{1,0:T(8,128)(2,1)} %param.9) | copy-start | bytes 786436
  272.2 211.0 %copy-start.6 = (bf16[1024,128]{1,0:T(8,128)(2,1)S(1)}, bf16[1024,128]{1,0:T(8,128)(2,1)}, u32[]{:S(2)}) copy-start(bf16[1024,128]{1,0:T(8,128)(2,1)} %param.10) | copy-start | bytes 786436
Sparse Core Ops, SparseCore 0:
  10.1 60.2 all-gather.6
  72.6 12.4 all-gather.8
  86.8 14.6 all-gather.10
  103.4 59.0 all-gather.12
  175.2 11.4 reduce-scatter.8
  189.6 13.6 reduce-scatter.10
  205.8 60.2 all-reduce.4
  269.7 77.6 reduce-scatter.14
  350.8 76.9 reduce-scatter.12
where the time goes:
time: 493 us; the launch traced here: 492 us
  waiting for transfers between devices  300 us (61%)
  blocking collectives  93.8 us (19%)
  matrix products  39 us (8%)
  other arithmetic  23.2 us (5%)
  local copies, waits for them, and re-layouts  21.3 us (4%)
  between operations  14.1 us (3%)
    unnamed x11, waiting for transfers between devices  156 us
    all_gather x1, waiting for transfers between devices, on_device(): lax.all_gather(cotangent, 'tp', axis=1, tiled=True)  61.1 us
    psum x1, blocking collectives, on_device(): sum_plain, sum_cross = lax.psum((sum_plain, sum_cross), 'tp')  38.7 us
    psum x1, waiting for transfers between devices, on_device(): lax.psum(shard_in.astype(jnp.bfloat16), 'rep').astype(jnp.float32)  30.6 us
    all_gather x1, blocking collectives, on_device(): lax.all_gather(ln_gain, 'tp', axis=0, tiled=True)  22.1 us
    unnamed x34, local copies, waits for them, and re-layouts  20 us
    all_gather x1, blocking collectives, on_device(): lax.all_gather(ln_bias, 'tp', axis=0, tiled=True)  19.5 us
    reduce_scatter x1, waiting for transfers between devices, on_device(): lax.psum_scatter(term_out.astype(jnp.bfloat16), 'fsdp', scatter_dimension...  16.6 us
  transfers between devices with their start and end apart: 9, of which 9 were waited for; matrix products, arithmetic and copies ran while one was open for 12% of the time, Pallas kernels for 0%

commit v1 on v0

--- a/solution.py
+++ b/solution.py
@@ -5,6 +5,28 @@
 from jax.sharding import PartitionSpec as P
 
 BLK = 128
+
+
+def in_order(blocks, dim):
+    shape = list(blocks.shape[1:])
+    shape[dim] *= blocks.shape[0]
+    return jnp.moveaxis(blocks, 0, dim).reshape(shape)
+
+
+def gather_around(x, axis, dim):
+    size = lax.axis_size(axis)
+    pairs = [(i, (i + 1) % size) for i in range(size)]
+    back = [(b, a) for a, b in pairs]
+    lower, upper = ([], [])
+    for step in range(size - 1):
+        if step % 2 == 0:
+            lower.append(lax.ppermute(lower[-1] if lower else x, axis, pairs))
+        else:
+            upper.append(lax.ppermute(upper[-1] if upper else x, axis, back))
+    tiles = jnp.stack([*lower[::-1], x, *upper])
+    shift = lax.axis_index(axis) - len(lower)
+    tiles = tiles[(jnp.arange(size) - shift) % size]
+    return in_order(tiles, dim)
 
 
 def apply_blocks(weight, blocks, kind):
@@ -33,7 +55,7 @@
         lax.all_gather(tokens, "tp", axis=1, tiled=True),
         lax.all_gather(cotangent, "tp", axis=1, tiled=True),
         lax.all_gather(ln_gain, "tp", axis=0, tiled=True),
-        lax.all_gather(ln_bias, "tp", axis=0, tiled=True),
+        gather_around(ln_bias, "tp", 0),
     )
     masked_in = apply_blocks(weight_in, blocks_in, jnp.bfloat16)
     masked_out = apply_blocks(weight_out, blocks_out, jnp.bfloat16)

time: 493 us -> 493 us (level)
  starting transfers between devices: 0.54 us -> 39.8 us
  blocking collectives: 93.8 us -> 72.3 us
  waiting for transfers between devices: 300 us -> 282 us
    ppermute x0 -> x15, starting transfers between devices: none -> 39.2 us  [the longest x7 37.5 us: gather_around(): upper.append(lax.ppermute(upper[-1] if upper else x, axis, back))]
    all_gather x1 -> x0, blocking collectives: 19.5 us -> none  [on_device(): lax.all_gather(ln_bias, 'tp', axis=0, tiled=True)]
    all_gather x1, waiting for transfers between devices: 14.8 us -> 0.02 us  [on_device(): lax.all_gather(tokens, 'tp', axis=1, tiled=True)]
    ppermute x0 -> x15, waiting for transfers between devices: none -> 10.1 us  [the longest x8 10.1 us: gather_around(): lower.append(lax.ppermute(lower[-1] if lower else x, axis, pairs))]
    all_gather x1, waiting for transfers between devices: 10.1 us -> 0.02 us  [on_device(): lax.all_gather(masked_in, 'fsdp', axis=0, tiled=True)]
  transfers between devices with their start and end apart: 9 -> 24, of which waited for: 9 -> 14; matrix products, arithmetic and copies ran while one was open for 12% -> 13% of each run, Pallas kernels for 0% -> 0%
where the time goes in v1:
time: 493 us; the launch traced here: 492 us
  waiting for transfers between devices  282 us (57%)
  blocking collectives  72.3 us (15%)
  starting transfers between devices  39.8 us (8%)
  matrix products  39.1 us (8%)
  other arithmetic  23.2 us (5%)
  local copies, waits for them, and re-layouts  21.9 us (4%)
  between operations  14.1 us (3%)
    unnamed x11, waiting for transfers between devices  156 us
    all_gather x1, waiting for transfers between devices, on_device(): lax.all_gather(cotangent, 'tp', axis=1, tiled=True)  61.1 us
    psum x1, blocking collectives, on_device(): sum_plain, sum_cross = lax.psum((sum_plain, sum_cross), 'tp')  38.7 us
    ppermute x7, starting transfers between devices, gather_around(): upper.append(lax.ppermute(upper[-1] if upper else x, axis, back))  37.5 us
    psum x1, waiting for transfers between devices, on_device(): lax.psum(shard_in.astype(jnp.bfloat16), 'rep').astype(jnp.float32)  30.6 us
    all_gather x1, blocking collectives, on_device(): lax.all_gather(ln_gain, 'tp', axis=0, tiled=True)  20.1 us
    unnamed x34, local copies, waits for them, and re-layouts  20 us
    reduce_scatter x1, waiting for transfers between devices, on_device(): lax.psum_scatter(term_out.astype(jnp.bfloat16), 'fsdp', scatter_dimension...  16.6 us
  transfers between devices with their start and end apart: 24, of which 14 were waited for; matrix products, arithmetic and copies ran while one was open for 13% of the time, Pallas kernels for 0%

profile of v1, /device:TPU:0, one launch (start us, length us, event | category | flops | bytes accessed | tf_op | source)
XLA Modules:
  0.0 492.0 jit_solution(7356385947162483297)
XLA Ops:
  7.2 0.7 all-gather.6.cloned.1.call-update
  7.9 0.8 fusion.36
  8.7 0.1 copy.17
  8.8 0.3 mul.149
  9.2 2.4 bitcast_multiply_fusion.3
  11.6 0.0 all-gather.10.cloned.1.call-start
  11.7 0.2 mul.155
  12.0 1.2 bitcast_multiply_fusion.2
  13.2 0.5 all-gather.12.cloned.1.call-update
  13.8 1.7 collective-permute-start
  15.5 5.0 %collective-permute-start.8 = (bf16[128]{0:T(256)(128)(2,1)S(1)}, bf16[128]{0:T(256)(128)(2,1)S(1)}, u32[]{:S(2)}, u32[]{:S(2)}) collective-permute-start(bf16[128]{0:T(256)(128)(2,1)S(1)} %copy-done.9), channel_id=1, source_target_pairs={{1,0},{2,1},{3,2},{4,3},{5,4},{6,5},{7,6},{8,7},{9,8},{10,9},{11,1... | collective-permute-start | bytes 776 | tf_op jit(solution)/shard_map/ppermute | solution.py:25
  20.5 1.4 collective-permute-done
  22.0 5.4 %collective-permute-start.9 = (bf16[128]{0:T(256)(128)(2,1)S(1)}, bf16[128]{0:T(256)(128)(2,1)S(1)}, u32[]{:S(2)}, u32[]{:S(2)}) collective-permute-start(bf16[128]{0:T(256)(128)(2,1)S(1)} %collective-permute-done.8), channel_id=1, source_target_pairs={{1,0},{2,1},{3,2},{4,3},{5,4},{6,5},{7,6},{8,7},{9,8},{10,9},{11,1... | collective-permute-start | bytes 776 | tf_op jit(solution)/shard_map/ppermute | solution.py:25
  27.4 1.4 collective-permute-done.1
  28.8 5.4 %collective-permute-start.10 = (bf16[128]{0:T(256)(128)(2,1)S(1)}, bf16[128]{0:T(256)(128)(2,1)S(1)}, u32[]{:S(2)}, u32[]{:S(2)}) collective-permute-start(bf16[128]{0:T(256)(128)(2,1)S(1)} %collective-permute-done.9), channel_id=1, source_target_pairs={{1,0},{2,1},{3,2},{4,3},{5,4},{6,5},{7,6},{8,7},{9,8},{10,9},{11,1... | collective-permute-start | bytes 776 | tf_op jit(solution)/shard_map/ppermute | solution.py:25
  34.2 1.4 collective-permute-done.2
  35.7 5.4 %collective-permute-start.11 = (bf16[128]{0:T(256)(128)(2,1)S(1)}, bf16[128]{0:T(256)(128)(2,1)S(1)}, u32[]{:S(2)}, u32[]{:S(2)}) collective-permute-start(bf16[128]{0:T(256)(128)(2,1)S(1)} %collective-permute-done.10), channel_id=1, source_target_pairs={{1,0},{2,1},{3,2},{4,3},{5,4},{6,5},{7,6},{8,7},{9,8},{10,9},{11,1... | collective-permute-start | bytes 776 | tf_op jit(solution)/shard_map/ppermute | solution.py:25
  41.1 1.4 collective-permute-done.3
  42.5 5.4 %collective-permute-start.12 = (bf16[128]{0:T(256)(128)(2,1)S(1)}, bf16[128]{0:T(256)(128)(2,1)S(1)}, u32[]{:S(2)}, u32[]{:S(2)}) collective-permute-start(bf16[128]{0:T(256)(128)(2,1)S(1)} %collective-permute-done.11), channel_id=1, source_target_pairs={{1,0},{2,1},{3,2},{4,3},{5,4},{6,5},{7,6},{8,7},{9,8},{10,9},{11,1... | collective-permute-start | bytes 776 | tf_op jit(solution)/shard_map/ppermute | solution.py:25
  48.0 1.4 collective-permute-done.4
  49.4 5.4 %collective-permute-start.13 = (bf16[128]{0:T(256)(128)(2,1)S(1)}, bf16[128]{0:T(256)(128)(2,1)S(1)}, u32[]{:S(2)}, u32[]{:S(2)}) collective-permute-start(bf16[128]{0:T(256)(128)(2,1)S(1)} %collective-permute-done.12), channel_id=1, source_target_pairs={{1,0},{2,1},{3,2},{4,3},{5,4},{6,5},{7,6},{8,7},{9,8},{10,9},{11,1... | collective-permute-start | bytes 776 | tf_op jit(solution)/shard_map/ppermute | solution.py:25
  54.8 1.4 collective-permute-done.5
  56.3 5.4 %collective-permute-start.14 = (bf16[128]{0:T(256)(128)(2,1)S(1)}, bf16[128]{0:T(256)(128)(2,1)S(1)}, u32[]{:S(2)}, u32[]{:S(2)}) collective-permute-start(bf16[128]{0:T(256)(128)(2,1)S(1)} %collective-permute-done.13), channel_id=1, source_target_pairs={{1,0},{2,1},{3,2},{4,3},{5,4},{6,5},{7,6},{8,7},{9,8},{10,9},{11,1... | collective-permute-start | bytes 776 | tf_op jit(solution)/shard_map/ppermute | solution.py:25
  61.7 1.4 collective-permute-done.6
  63.1 20.1 %all-gather = bf16[16,1,128]{2,1,0:T(2,128)(2,1)S(1)} all-gather(bf16[1,1,128]{2,1,0:T(2,128)(2,1)S(1)} %bitcast.62), channel_id=1, replica_groups=mesh['rep'=4,'fsdp'=2,'tp'=16] {'tp'}, dimensions={0}, use_global_device_ids=true | all-gather | bytes 4352 | tf_op jit(solution)/shard_map/all_gather | solution.py:57
  83.3 0.1 stack.67
  83.4 0.6 gather_fusion
  84.0 3.0 convert_reduce_fusion
  87.0 0.5 copy-done
  87.5 1.2 fusion.2
  88.7 10.5 %multiply_convert_fusion = (bf16[1024,512]{1,0:T(8,128)(2,1)S(1)}, f32[1024,512]{1,0:T(8,128)}, f32[1024,512]{1,0:T(8,128)}) fusion(bf16[2048,512]{1,0:T(8,128)(2,1)} %all-gather.8.cloned.1.call-done, f32[2048]{0:T(1024)S(1)} %bitcast_convert_fusion, f32[2048]{0:T(1024)S(1)} %bitcast.59, f32[1024]{0:T(1024)S(1)} %add_rsqrt_fusion, ...), kind=kOutput, calls=%fused_computation.22 | convolution fusion | flops 2194145280 | bytes 11558912 | tf_op jit(solution)/shard_map/dot_general | solution.py:78
  99.2 2.2 all-gather.10.cloned.1.call-done
  101.4 61.1 %all-gather.12.cloned.1.call-done = bf16[1024,2048]{1,0:T(8,128)(2,1)} async-done(((bf16[1024,128]{1,0:T(8,128)(2,1)}), bf16[1024,2048]{1,0:T(8,128)(2,1)}) %all-gather.12.cloned.1.call-update) | async-done | bytes 4194320 | tf_op jit(solution)/shard_map/all_gather | solution.py:56
  162.5 7.1 %add_convert_fusion.1 = bf16[1024,512]{1,0:T(8,128)(2,1)S(1)} fusion(f32[1024,512]{1,0:T(8,128)} %get-tuple-element.17, f32[1024,512]{1,0:T(8,128)} %get-tuple-element.22, bf16[512,2048]{1,0:T(8,128)(2,1)} %all-gather.10.cloned.1.call-done, bf16[1024,2048]{1,0:T(8,128)(2,1)} %all-gather.12.cloned.1.call-done, bf16[1024]{0:T(1024)(128)(2,1)S(1)} %convert_element_type.96), kind=kOutput, calls=%fused_computation.19 | convolution fusion | flops 2156920832 | bytes 11536384 | tf_op jit(solution)/shard_map/dot_general | solution.py:46
  169.6 0.9 copy-done.14
  170.6 4.5 convolution_convert_fusion.2
  175.0 0.3 reduce-scatter.11.cloned.1.call-start
  175.3 6.0 %fusion.7 = bf16[512,2048]{1,0:T(8,128)(2,1)} fusion(bf16[1024,512]{1,0:T(8,128)(2,1)S(1)} %get-tuple-element.16, bf16[1024,2048]{1,0:T(8,128)(2,1)} %all-gather.12.cloned.1.call-done, bf16[1024]{0:T(1024)(128)(2,1)S(1)} %convert_element_type.96), kind=kOutput, calls=%fused_computation.15 | convolution fusion | flops 2150629376 | bytes 7342080 | tf_op jit(solution)/shard_map/dot_general | solution.py:40
  181.4 5.3 %reduce-scatter.9.cloned.1.call-done = bf16[1024,512]{1,0:T(8,128)(2,1)} async-done(((bf16[2048,512]{1,0:T(8,128)(2,1)}), bf16[1024,512]{1,0:T(8,128)(2,1)}) %reduce-scatter.9.cloned.1.call-update) | async-done | bytes 1048592 | tf_op jit(solution)/shard_map/reduce_scatter | solution.py:111
  186.6 16.6 %reduce-scatter.11.cloned.1.call-done = bf16[512,1024]{1,0:T(8,128)(2,1)} async-done(((bf16[512,2048]{1,0:T(8,128)(2,1)}), bf16[512,1024]{1,0:T(8,128)(2,1)}) %reduce-scatter.11.cloned.1.call-update) | async-done | bytes 1048592 | tf_op jit(solution)/shard_map/reduce_scatter | solution.py:114
  203.3 5.5 %convolution_convert_fusion = bf16[1024,2048]{1,0:T(8,128)(2,1)} fusion(bf16[1024,512]{1,0:T(8,128)(2,1)} %copy-done.14, bf16[2048,512]{1,0:T(8,128)(2,1)S(1)} %copy-done.11), kind=kOutput, calls=%fused_computation.7 | convolution fusion | flops 2149580800 | bytes 7340032 | tf_op jit(solution)/shard_map/dot_general | solution.py:46
  208.8 6.4 %copy.21 = bf16[1024,2048]{0,1:T(8,128)(2,1)} copy(bf16[1024,2048]{1,0:T(8,128)(2,1)} %convolution_convert_fusion) | data formatting | bytes 8388608
  215.2 0.0 reduce-scatter.13.cloned.1.call-start
  215.3 1.6 copy-done.12
  216.9 5.5 %convolution_convert_fusion.1 = bf16[1024,2048]{1,0:T(8,128)(2,1)} fusion(bf16[1024,512]{1,0:T(8,128)(2,1)} %copy-done.13, bf16[512,2048]{1,0:T(8,128)(2,1)S(1)} %copy-done.12), kind=kOutput, calls=%fused_computation.8 | convolution fusion | flops 2149580800 | bytes 7340032 | tf_op jit(solution)/shard_map/dot_general | solution.py:80
  222.4 6.4 %copy.19 = bf16[1024,2048]{0,1:T(8,128)(2,1)} copy(bf16[1024,2048]{1,0:T(8,128)(2,1)} %convolution_convert_fusion.1) | data formatting | bytes 8388608
  228.8 0.1 copy.18
  228.9 6.4 %fusion = f32[1024,2048]{1,0:T(8,128)} fusion(bf16[1024,2048]{1,0:T(8,128)(2,1)} %all-gather.6.cloned.1.call-done, f32[1024]{0:T(1024)S(1)} %add_rsqrt_fusion, f32[1024]{0:T(1024)S(1)} %broadcast_multiply_fusion.2), kind=kLoop, calls=%fused_computation.3 | loop fusion | flops 6291456 | bytes 12591104 | tf_op jit(solution)/shard_map/mul | solution.py:74
  235.3 30.6 %all-reduce.5.cloned.1.call-done = (bf16[1024,512]{1,0:T(8,128)(2,1)}, bf16[512,1024]{1,0:T(8,128)(2,1)}) async-done(((bf16[1024,512]{1,0:T(8,128)(2,1)}, bf16[512,1024]{1,0:T(8,128)(2,1)}), (bf16[1024,512]{1,0:T(8,128)(2,1)}, bf16[512,1024]{1,0:T(8,128)(2,1)})) %all-reduce.5.cloned.1.call-update) | async-done | bytes 2097168 | tf_op jit(solution)/shard_map/psum | solution.py:119
  265.9 0.3 mul.177
  266.3 0.9 copy-done.4
  267.2 1.7 bitcast_multiply_fusion.1
  268.9 0.2 mul.180
  269.1 1.0 copy-done.3
  270.1 2.0 bitcast_multiply_fusion
  272.1 75.3 %reduce-scatter.15.cloned.1.call-done = bf16[128,1024]{1,0:T(8,128)(2,1)} async-done(((bf16[2048,1024]{1,0:T(8,128)(2,1)}), bf16[128,1024]{1,0:T(8,128)(2,1)}) %reduce-scatter.15.cloned.1.call-update) | async-done | bytes 262160
  347.3 1.1 copy.22
  348.4 79.2 %reduce-scatter.13.cloned.1.call-done = bf16[128,1024]{1,0:T(8,128)(2,1)} async-done(((bf16[2048,1024]{1,0:T(8,128)(2,1)}), bf16[128,1024]{1,0:T(8,128)(2,1)}) %reduce-scatter.13.cloned.1.call-update) | async-done | bytes 262160
  427.6 1.1 copy.20
  428.8 0.8 add_convert_fusion.4
  429.5 1.4 fusion.29
  430.9 13.5 %all-reduce.1 = (f32[128]{0:T(128)}, f32[128]{0:T(128)}) all-reduce(f32[128]{0:T(128)S(1)} %get-tuple-element.6, f32[128]{0:T(128)S(1)} %get-tuple-element.9), channel_id=1, replica_groups=mesh['rep'=4,'fsdp'=2,'tp'=16] {'rep','fsdp'}, use_global_device_ids=true, to_apply=%region_13.14 | all-reduce | flops 256 | bytes 2048 | tf_op jit(solution)/shard_map/psum | solution.py:107
  444.4 38.7 %all-reduce = (f32[1024]{0:T(1024)S(1)}, f32[1024]{0:T(1024)S(1)}) all-reduce(f32[1024]{0:T(1024)S(1)} %get-tuple-element.7, f32[1024]{0:T(1024)S(1)} %get-tuple-element.8), channel_id=1, replica_groups=mesh['rep'=4,'fsdp'=2,'tp'=16] {'tp'}, use_global_device_ids=true, to_apply=%region_7.8 | all-reduce | flops 2048 | bytes 16384 | tf_op jit(solution)/shard_map/psum | solution.py:100
  483.1 2.4 fusion.27
  (65 shorter events, 0.6 us)
Async XLA Ops:
  7.2 76.8 %all-gather.6.cloned.1.call-start = ((), (), s32[]{:S(2)}) async-start(), calls=%async_computation.4 | async-start | bytes 4456448 | tf_op jit(solution)/shard_map/all_gather | solution.py:55
  7.9 80.8 %all-gather.8.cloned.1.call-start = ((), (), s32[]{:S(2)}) async-start(), calls=%async_computation.5 | async-start | bytes 3145728 | tf_op jit(solution)/shard_map/all_gather | solution.py:63
  9.2 2.5 copy-start.8
  9.2 2.7 copy-start.2
  11.6 89.8 %all-gather.10.cloned.1.call-start = ((), (), s32[]{:S(2)}) async-start(), calls=%async_computation.6 | async-start | bytes 3145728 | tf_op jit(solution)/shard_map/all_gather | solution.py:64
  11.9 1.9 copy-start.9
  11.9 51.2 %copy-start.10 = (bf16[128]{0:T(256)(128)(2,1)S(1)}, bf16[128]{0:T(256)(128)(2,1)}, u32[]{:S(2)}) copy-start(bf16[128]{0:T(256)(128)(2,1)} %param.12) | copy-start | bytes 772
  11.9 71.3 %copy-start.7 = (s32[1024]{0:T(1024)S(1)}, s32[1024]{0:T(1024)}, u32[]{:S(2)}) copy-start(s32[1024]{0:T(1024)} %param.11) | copy-start | bytes 12292
  13.1 149.3 %all-gather.12.cloned.1.call-start = ((), (), s32[]{:S(2)}) async-start(), calls=%async_computation.7 | async-start | bytes 4456448 | tf_op jit(solution)/shard_map/all_gather | solution.py:56
  13.7 172.9 %reduce-scatter.9.cloned.1.call-start = ((), (), s32[]{:S(2)}) async-start(), calls=%async_computation.8 | async-start | bytes 3145728 | tf_op jit(solution)/shard_map/reduce_scatter | solution.py:111
  13.8 8.2 %collective-permute-start = (bf16[128]{0:T(256)(128)(2,1)S(1)}, bf16[128]{0:T(256)(128)(2,1)S(1)}, u32[]{:S(2)}, u32[]{:S(2)}) collective-permute-start(bf16[128]{0:T(256)(128)(2,1)S(1)} %copy-done.9), channel_id=1, source_target_pairs={{0,1},{1,2},{2,3},{3,4},{4,5},{5,6},{6,7},{7,8},{8,9},{9,10},{10,1... | collective-permute-start | bytes 776 | tf_op jit(solution)/shard_map/ppermute | solution.py:23
  15.5 6.4 %collective-permute-start.8 = (bf16[128]{0:T(256)(128)(2,1)S(1)}, bf16[128]{0:T(256)(128)(2,1)S(1)}, u32[]{:S(2)}, u32[]{:S(2)}) collective-permute-start(bf16[128]{0:T(256)(128)(2,1)S(1)} %copy-done.9), channel_id=1, source_target_pairs={{1,0},{2,1},{3,2},{4,3},{5,4},{6,5},{7,6},{8,7},{9,8},{10,9},{11,1... | collective-permute-start | bytes 776 | tf_op jit(solution)/shard_map/ppermute | solution.py:25
  21.9 6.9 %collective-permute-start.1 = (bf16[128]{0:T(256)(128)(2,1)S(1)}, bf16[128]{0:T(256)(128)(2,1)S(1)}, u32[]{:S(2)}, u32[]{:S(2)}) collective-permute-start(bf16[128]{0:T(256)(128)(2,1)S(1)} %collective-permute-done), channel_id=1, source_target_pairs={{0,1},{1,2},{2,3},{3,4},{4,5},{5,6},{6,7},{7,8},{8,9},{9,10},{10,1... | collective-permute-start | bytes 776 | tf_op jit(solution)/shard_map/ppermute | solution.py:23
  22.0 6.9 %collective-permute-start.9 = (bf16[128]{0:T(256)(128)(2,1)S(1)}, bf16[128]{0:T(256)(128)(2,1)S(1)}, u32[]{:S(2)}, u32[]{:S(2)}) collective-permute-start(bf16[128]{0:T(256)(128)(2,1)S(1)} %collective-permute-done.8), channel_id=1, source_target_pairs={{1,0},{2,1},{3,2},{4,3},{5,4},{6,5},{7,6},{8,7},{9,8},{10,9},{11,1... | collective-permute-start | bytes 776 | tf_op jit(solution)/shard_map/ppermute | solution.py:25
  28.8 6.9 %collective-permute-start.2 = (bf16[128]{0:T(256)(128)(2,1)S(1)}, bf16[128]{0:T(256)(128)(2,1)S(1)}, u32[]{:S(2)}, u32[]{:S(2)}) collective-permute-start(bf16[128]{0:T(256)(128)(2,1)S(1)} %collective-permute-done.1), channel_id=1, source_target_pairs={{0,1},{1,2},{2,3},{3,4},{4,5},{5,6},{6,7},{7,8},{8,9},{9,10},{10,1... | collective-permute-start | bytes 776 | tf_op jit(solution)/shard_map/ppermute | solution.py:23
  28.8 6.9 %collective-permute-start.10 = (bf16[128]{0:T(256)(128)(2,1)S(1)}, bf16[128]{0:T(256)(128)(2,1)S(1)}, u32[]{:S(2)}, u32[]{:S(2)}) collective-permute-start(bf16[128]{0:T(256)(128)(2,1)S(1)} %collective-permute-done.9), channel_id=1, source_target_pairs={{1,0},{2,1},{3,2},{4,3},{5,4},{6,5},{7,6},{8,7},{9,8},{10,9},{11,1... | collective-permute-start | bytes 776 | tf_op jit(solution)/shard_map/ppermute | solution.py:25
  35.7 6.9 %collective-permute-start.3 = (bf16[128]{0:T(256)(128)(2,1)S(1)}, bf16[128]{0:T(256)(128)(2,1)S(1)}, u32[]{:S(2)}, u32[]{:S(2)}) collective-permute-start(bf16[128]{0:T(256)(128)(2,1)S(1)} %collective-permute-done.2), channel_id=1, source_target_pairs={{0,1},{1,2},{2,3},{3,4},{4,5},{5,6},{6,7},{7,8},{8,9},{9,10},{10,1... | collective-permute-start | bytes 776 | tf_op jit(solution)/shard_map/ppermute | solution.py:23
  35.7 6.9 %collective-permute-start.11 = (bf16[128]{0:T(256)(128)(2,1)S(1)}, bf16[128]{0:T(256)(128)(2,1)S(1)}, u32[]{:S(2)}, u32[]{:S(2)}) collective-permute-start(bf16[128]{0:T(256)(128)(2,1)S(1)} %collective-permute-done.10), channel_id=1, source_target_pairs={{1,0},{2,1},{3,2},{4,3},{5,4},{6,5},{7,6},{8,7},{9,8},{10,9},{11,1... | collective-permute-start | bytes 776 | tf_op jit(solution)/shard_map/ppermute | solution.py:25
  42.5 6.9 %collective-permute-start.4 = (bf16[128]{0:T(256)(128)(2,1)S(1)}, bf16[128]{0:T(256)(128)(2,1)S(1)}, u32[]{:S(2)}, u32[]{:S(2)}) collective-permute-start(bf16[128]{0:T(256)(128)(2,1)S(1)} %collective-permute-done.3), channel_id=1, source_target_pairs={{0,1},{1,2},{2,3},{3,4},{4,5},{5,6},{6,7},{7,8},{8,9},{9,10},{10,1... | collective-permute-start | bytes 776 | tf_op jit(solution)/shard_map/ppermute | solution.py:23
  42.5 6.9 %collective-permute-start.12 = (bf16[128]{0:T(256)(128)(2,1)S(1)}, bf16[128]{0:T(256)(128)(2,1)S(1)}, u32[]{:S(2)}, u32[]{:S(2)}) collective-permute-start(bf16[128]{0:T(256)(128)(2,1)S(1)} %collective-permute-done.11), channel_id=1, source_target_pairs={{1,0},{2,1},{3,2},{4,3},{5,4},{6,5},{7,6},{8,7},{9,8},{10,9},{11,1... | collective-permute-start | bytes 776 | tf_op jit(solution)/shard_map/ppermute | solution.py:25
  49.4 6.9 %collective-permute-start.5 = (bf16[128]{0:T(256)(128)(2,1)S(1)}, bf16[128]{0:T(256)(128)(2,1)S(1)}, u32[]{:S(2)}, u32[]{:S(2)}) collective-permute-start(bf16[128]{0:T(256)(128)(2,1)S(1)} %collective-permute-done.4), channel_id=1, source_target_pairs={{0,1},{1,2},{2,3},{3,4},{4,5},{5,6},{6,7},{7,8},{8,9},{9,10},{10,1... | collective-permute-start | bytes 776 | tf_op jit(solution)/shard_map/ppermute | solution.py:23
  49.4 6.9 %collective-permute-start.13 = (bf16[128]{0:T(256)(128)(2,1)S(1)}, bf16[128]{0:T(256)(128)(2,1)S(1)}, u32[]{:S(2)}, u32[]{:S(2)}) collective-permute-start(bf16[128]{0:T(256)(128)(2,1)S(1)} %collective-permute-done.12), channel_id=1, source_target_pairs={{1,0},{2,1},{3,2},{4,3},{5,4},{6,5},{7,6},{8,7},{9,8},{10,9},{11,1... | collective-permute-start | bytes 776 | tf_op jit(solution)/shard_map/ppermute | solution.py:25
  56.3 6.9 %collective-permute-start.6 = (bf16[128]{0:T(256)(128)(2,1)S(1)}, bf16[128]{0:T(256)(128)(2,1)S(1)}, u32[]{:S(2)}, u32[]{:S(2)}) collective-permute-start(bf16[128]{0:T(256)(128)(2,1)S(1)} %collective-permute-done.5), channel_id=1, source_target_pairs={{0,1},{1,2},{2,3},{3,4},{4,5},{5,6},{6,7},{7,8},{8,9},{9,10},{10,1... | collective-permute-start | bytes 776 | tf_op jit(solution)/shard_map/ppermute | solution.py:23
  56.3 27.0 %collective-permute-start.14 = (bf16[128]{0:T(256)(128)(2,1)S(1)}, bf16[128]{0:T(256)(128)(2,1)S(1)}, u32[]{:S(2)}, u32[]{:S(2)}) collective-permute-start(bf16[128]{0:T(256)(128)(2,1)S(1)} %collective-permute-done.13), channel_id=1, source_target_pairs={{1,0},{2,1},{3,2},{4,3},{5,4},{6,5},{7,6},{8,7},{9,8},{10,9},{11,1... | collective-permute-start | bytes 776 | tf_op jit(solution)/shard_map/ppermute | solution.py:25
  63.1 20.2 %collective-permute-start.7 = (bf16[128]{0:T(256)(128)(2,1)S(1)}, bf16[128]{0:T(256)(128)(2,1)S(1)}, u32[]{:S(2)}, u32[]{:S(2)}) collective-permute-start(bf16[128]{0:T(256)(128)(2,1)S(1)} %collective-permute-done.6), channel_id=1, source_target_pairs={{0,1},{1,2},{2,3},{3,4},{4,5},{5,6},{6,7},{7,8},{8,9},{9,10},{10,1... | collective-permute-start | bytes 776 | tf_op jit(solution)/shard_map/ppermute | solution.py:23
  84.0 3.5 copy-start
  99.2 76.1 %copy-start.13 = (bf16[1024,512]{1,0:T(8,128)(2,1)}, bf16[1024,512]{1,0:T(8,128)(2,1)S(1)}, u32[]{:S(2)}) copy-start(bf16[1024,512]{1,0:T(8,128)(2,1)S(1)} %get-tuple-element.16) | copy-start | bytes 3145732
  162.5 8.1 %copy-start.1 = (bf16[1024,2048]{1,0:T(8,128)(2,1)S(1)}, bf16[1024,2048]{1,0:T(8,128)(2,1)}, u32[]{:S(2)}) copy-start(bf16[1024,2048]{1,0:T(8,128)(2,1)} %all-gather.6.cloned.1.call-done) | copy-start | bytes 12582916
  169.6 1.0 copy-start.14
  175.0 28.2 %reduce-scatter.11.cloned.1.call-start = ((), (), s32[]{:S(2)}) async-start(), calls=%async_computation.9 | async-start | bytes 3145728 | tf_op jit(solution)/shard_map/reduce_scatter | solution.py:114
  181.3 22.0 %copy-start.11 = (bf16[2048,512]{1,0:T(8,128)(2,1)S(1)}, bf16[2048,512]{1,0:T(8,128)(2,1)}, u32[]{:S(2)}) copy-start(bf16[2048,512]{1,0:T(8,128)(2,1)} %all-gather.8.cloned.1.call-done) | copy-start | bytes 6291460
  181.3 84.6 %all-reduce.5.cloned.1.call-start = ((), (), s32[]{:S(2)}) async-start(), calls=%async_computation.12 | async-start | bytes 4194304 | tf_op jit(solution)/shard_map/psum | solution.py:119
  203.2 144.1 %reduce-scatter.15.cloned.1.call-start = ((), (), s32[]{:S(2)}) async-start(), calls=%async_computation.11 | async-start | bytes 4456448
  215.2 1.6 copy-start.12
  215.2 212.4 %reduce-scatter.13.cloned.1.call-start = ((), (), s32[]{:S(2)}) async-start(), calls=%async_computation.10 | async-start | bytes 4456448
  265.9 1.2 copy-start.4
  268.9 1.2 copy-start.3
  270.1 158.7 %copy-start.5 = (bf16[1024,128]{1,0:T(8,128)(2,1)S(1)}, bf16[1024,128]{1,0:T(8,128)(2,1)}, u32[]{:S(2)}) copy-start(bf16[1024,128]{1,0:T(8,128)(2,1)} %param.9) | copy-start | bytes 786436
  272.1 211.0 %copy-start.6 = (bf16[1024,128]{1,0:T(8,128)(2,1)S(1)}, bf16[1024,128]{1,0:T(8,128)(2,1)}, u32[]{:S(2)}) copy-start(bf16[1024,128]{1,0:T(8,128)(2,1)} %param.10) | copy-start | bytes 786436
Sparse Core Ops, SparseCore 0:
  10.1 60.2 all-gather.5
  72.6 12.4 all-gather.7
  86.7 14.6 all-gather.9
  103.4 59.0 all-gather.11
  175.2 11.4 reduce-scatter.8
  189.5 13.6 reduce-scatter.10
  205.7 60.2 all-reduce.4
  269.6 77.6 reduce-scatter.14
  350.7 76.9 reduce-scatter.12
